TPU v7x, 128 devices: a whole 4x4x4 slice. The times are simulated.
128 devices in a mesh: space: 32 (over x, z, core), feat: 4 (over y).
Axes of the slice: x: 4, y: 4, z: 4, core: 2. Of those that a mesh axis runs over, the one named last changes fastest.
Arguments:
- inputs: bfloat16 [2, 96, 180, 1024], P(None, 'space', None, 'feat'), may hold values from -15 to 15
- cotangent: bfloat16 [2, 96, 180, 1024], P(None, 'space', None, 'feat'), may hold values from -6 to 6
- spec_w1: float32 [2, 8, 128, 128], P(None, 'feat'), may hold values from -0.375 to 0.375
- spec_b1: float32 [2, 1024], P(None, 'feat'), may hold values from -0.3 to 0.3
- spec_w2: float32 [2, 8, 128, 128], P(None, 'feat'), may hold values from -0.375 to 0.375
- spec_b2: float32 [2, 1024], P(None, 'feat'), may hold values from -0.3 to 0.3
- up_weight: bfloat16 [1024, 4096], P(None, 'feat'), may hold values from -0.1875 to 0.1875
- down_weight: bfloat16 [4096, 1024], P('feat'), may hold values from -0.09375 to 0.09375
Outputs:
- output: bfloat16 [2, 96, 180, 1024], P(None, 'space', None, 'feat')
- grad_input: bfloat16 [2, 96, 180, 1024], P(None, 'space', None, 'feat')
All inputs are finite; a program needn't handle non-finite values.
Results may differ from a plain program's by a relative error of at most 0.0102.
Values may be sent and summed in bfloat16 or wider, within the bound.
No kernel may reach another device: no remote copies, remote signals or barrier semaphores. Data moves between devices by JAX's collectives and lax.ppermute only.
A program may use at most 128 MiB of HBM per device.

v0:
```python
import math
import jax
import jax.numpy as jnp
from jax import lax
from jax.sharding import PartitionSpec as P

EPSILON = 1e-05
SHRINK_LEVEL = 0.1
HIGHEST = lax.Precision.HIGHEST


def longitude_tables(width_lon):
    mode_count = width_lon // 2 + 1
    cell_index = jnp.arange(width_lon, dtype=jnp.int32)[:, None]
    wave_number = jnp.arange(mode_count, dtype=jnp.int32)[None, :]
    phase_angle = (
        2.0 * math.pi / width_lon * (cell_index * wave_number % width_lon).astype(jnp.float32)
    )
    scaling = 1.0 / math.sqrt(width_lon)
    cos_fwd = jnp.cos(phase_angle) * scaling
    sin_fwd = -jnp.sin(phase_angle) * scaling
    doubled = jnp.where((wave_number == 0) | (wave_number * 2 == width_lon), 1.0, 2.0).astype(
        jnp.float32
    )
    return (cos_fwd, sin_fwd, cos_fwd * doubled, sin_fwd * doubled)


def padded_tables(width_lon, multiple):
    tables = longitude_tables(width_lon)
    modes = tables[0].shape[1]
    extra = -modes % multiple
    return tuple((jnp.pad(table, ((0, 0), (0, extra))) for table in tables))


def lat_apply(table, field):
    return jnp.einsum("gh,bhkc->bgkc", table, field, precision=HIGHEST)


def complex_latitude(table_cos, table_sin, real_part, imag_part, inverse):
    if inverse:
        return (
            lat_apply(table_cos, real_part) + lat_apply(table_sin, imag_part),
            lat_apply(table_cos, imag_part) - lat_apply(table_sin, real_part),
        )
    return (
        lat_apply(table_cos, real_part) - lat_apply(table_sin, imag_part),
        lat_apply(table_cos, imag_part) + lat_apply(table_sin, real_part),
    )


def lon_forward(field, table):
    return jnp.einsum("brwc,wk->brkc", field, table, precision=HIGHEST)


def lon_back(spec, table):
    return jnp.einsum("brkc,wk->brwc", spec, table, precision=HIGHEST)


def to_blocks(field, block_size):
    return field.reshape(field.shape[:-1] + (field.shape[-1] // block_size, block_size))


def block_mult(field, weights):
    return jnp.einsum("...nc,nce->...ne", field, weights, precision=HIGHEST)


def block_mult_back(field, weights):
    return jnp.einsum("...ne,nce->...nc", field, weights, precision=HIGHEST)


def block_product(real_part, imag_part, weights):
    return (
        block_mult(real_part, weights[0]) - block_mult(imag_part, weights[1]),
        block_mult(real_part, weights[1]) + block_mult(imag_part, weights[0]),
    )


def block_adjoint(real_part, imag_part, weights):
    return (
        block_mult_back(real_part, weights[0]) + block_mult_back(imag_part, weights[1]),
        block_mult_back(imag_part, weights[0]) - block_mult_back(real_part, weights[1]),
    )


def latitude_tables(length):
    index_row = jnp.arange(length, dtype=jnp.int32)
    phase_angle = (
        2.0
        * math.pi
        / length
        * (index_row[:, None] * index_row[None, :] % length).astype(jnp.float32)
    )
    scaling = 1.0 / math.sqrt(length)
    return (jnp.cos(phase_angle) * scaling, -jnp.sin(phase_angle) * scaling)


def to_columns(real_part, imag_part, link_type):
    stacked = jnp.stack([real_part, imag_part]).astype(link_type)
    moved = lax.all_to_all(stacked, "space", 3, 2, tiled=True).astype(jnp.float32)
    return (moved[0], moved[1])


def to_rows(real_part, imag_part, link_type):
    stacked = jnp.stack([real_part, imag_part]).astype(link_type)
    moved = lax.all_to_all(stacked, "space", 2, 3, tiled=True).astype(jnp.float32)
    return (moved[0], moved[1])


def enter_spectrum(real_part, imag_part, tables_lat, link_type=jnp.float32):
    table_cos, table_sin = tables_lat
    real_part, imag_part = to_columns(real_part, imag_part, link_type)
    return complex_latitude(table_cos, table_sin, real_part, imag_part, False)


def leave_spectrum(real_part, imag_part, tables_lat, link_type=jnp.float32):
    table_cos, table_sin = tables_lat
    real_part, imag_part = complex_latitude(table_cos, table_sin, real_part, imag_part, True)
    return to_rows(real_part, imag_part, link_type)


def complex_operator(real_block, imag_block):
    return jnp.stack([jnp.stack([real_block, -imag_block]), jnp.stack([imag_block, real_block])])


def lat_stacked(operator, field, precision=lax.Precision.HIGH):
    return jnp.einsum("pqkh,qbhlc->pbklc", operator, field, precision=precision)


def lon_stacked_forward(field, tables, precision=lax.Precision.HIGH):
    return jnp.einsum("brwc,pwk->pbrkc", field, tables, precision=precision)


def lon_stacked_back(spec, tables, precision=lax.Precision.HIGH):
    return jnp.einsum("pbrkc,pwk->brwc", spec, tables, precision=precision)


def block_operator(weights):
    return jnp.moveaxis(complex_operator(weights[0], weights[1]), 2, 0)


def block_stacked(field, operator):
    return jnp.einsum("qbklnc,npqce->pbklne", field, operator, precision=lax.Precision.HIGH)


def block_stacked_adjoint(field, operator):
    return jnp.einsum("pbklne,npqce->qbklnc", field, operator, precision=lax.Precision.DEFAULT)


def stacked_columns(field, link_type):
    return lax.all_to_all(field.astype(link_type), "space", 3, 2, tiled=True).astype(jnp.float32)


def stacked_rows(field, link_type):
    return lax.all_to_all(field.astype(link_type), "space", 2, 3, tiled=True).astype(jnp.float32)


def token_sums(first_term, second_term):
    pair = jnp.stack([first_term, second_term])
    count = lax.axis_size("feat")
    shifted = jnp.stack(
        [pair]
        + [
            lax.ppermute(pair, "feat", [(i, (i + count - shift) % count) for i in range(count)])
            for shift in range(1, count)
        ]
    )
    total = shifted[0]
    for source in range(1, count):
        total = total + shifted[source]
    return (total[0], total[1])


def ring_send(block):
    count = lax.axis_size("feat")
    return [block] + [
        lax.ppermute(block, "feat", [(i, (i + shift) % count) for i in range(count)])
        for shift in range(1, count)
    ]


def ring_assemble(parts):
    count = len(parts)
    position = lax.axis_index("feat")
    block = parts[0]
    width = block.shape[-1]
    whole = jnp.zeros(block.shape[:-1] + (width * count,), block.dtype)
    for shift, moved in enumerate(parts):
        source = (position + count - shift) % count
        whole = lax.dynamic_update_slice_in_dim(whole, moved, source * width, axis=block.ndim - 1)
    return whole


def channel_share(term):
    return lax.psum_scatter(
        term.astype(jnp.bfloat16), "feat", scatter_dimension=3, tiled=True
    ).astype(jnp.float32)


def gelu_value(field):
    return 0.5 * field * (1.0 + lax.erf(field * (1.0 / math.sqrt(2.0))))


def gelu_slope(field):
    return 0.5 * (1.0 + lax.erf(field * (1.0 / math.sqrt(2.0)))) + field * jnp.exp(
        -0.5 * field * field
    ) * (1.0 / math.sqrt(2.0 * math.pi))


def per_device(inputs, cotangent, spec_w1, spec_b1, spec_w2, spec_b2, up_weight, down_weight):
    full_width = up_weight.shape[0]
    block_size = spec_w1.shape[2]
    tables_lon = padded_tables(inputs.shape[2], lax.axis_size("space"))
    tables_lat = latitude_tables(inputs.shape[1] * lax.axis_size("space"))
    cos_fwd, sin_fwd, cos_inv, sin_inv = tables_lon
    table_cos, table_sin = tables_lat
    operators = (
        jnp.stack([cos_fwd, sin_fwd]),
        jnp.stack([cos_inv, sin_inv]),
        complex_operator(table_cos, table_sin),
        complex_operator(table_cos, -table_sin),
        block_operator(spec_w1),
        block_operator(spec_w2),
    )
    operators = lax.optimization_barrier(operators)
    lon_fwd_tables, lon_inv_tables, lat_forward_op, lat_inverse_op, first_op, second_op = operators
    values = inputs.astype(jnp.float32)
    cotangent_parts = lax.all_gather(cotangent, "feat", axis=3, tiled=True)
    first_sum, second_sum = token_sums(jnp.sum(values, axis=-1), jnp.sum(values * values, axis=-1))
    mean_one = first_sum[..., None] / full_width
    rstd_one = lax.rsqrt(second_sum[..., None] / full_width - mean_one * mean_one + EPSILON)
    normed = (values - mean_one) * rstd_one
    spec = lat_stacked(
        lat_forward_op, stacked_columns(lon_stacked_forward(normed, lon_fwd_tables), jnp.float32)
    )
    spec_blocks = to_blocks(spec, block_size)
    bias_one = to_blocks(spec_b1, block_size)[:, None, None, None]
    bias_two = to_blocks(spec_b2, block_size)[:, None, None, None]
    first = jax.nn.relu(block_stacked(spec_blocks, first_op) + bias_one)
    second = block_stacked(first, second_op) + bias_two
    shrunk = (second - jnp.clip(second, -SHRINK_LEVEL, SHRINK_LEVEL)).reshape(spec.shape)
    shrunk, cotangent_parts = lax.optimization_barrier((shrunk, cotangent_parts))
    whole_cotangent = cotangent_parts
    filtered = lon_stacked_back(
        stacked_rows(lat_stacked(lat_inverse_op, shrunk, lax.Precision.DEFAULT), jnp.bfloat16),
        lon_inv_tables,
        lax.Precision.DEFAULT,
    )
    residual = (filtered + normed + values).astype(jnp.bfloat16)
    residual_vals = residual.astype(jnp.float32)
    whole_residual = lax.all_gather(residual, "feat", axis=3, tiled=True)
    grad_act = jnp.einsum(
        "brwd,hd->brwh", whole_cotangent, down_weight, preferred_element_type=jnp.float32
    )
    whole_residual, grad_act = lax.optimization_barrier((whole_residual, grad_act))
    whole_vals = whole_residual.astype(jnp.float32)
    mean_two = jnp.sum(whole_vals, axis=-1, keepdims=True) / full_width
    square_two = jnp.sum(whole_vals * whole_vals, axis=-1, keepdims=True) / full_width
    rstd_two = lax.rsqrt(square_two - mean_two * mean_two + EPSILON)
    vhat = (whole_vals - mean_two) * rstd_two
    hidden = jnp.einsum(
        "brwd,dh->brwh", vhat.astype(jnp.bfloat16), up_weight, preferred_element_type=jnp.float32
    )
    activated = gelu_value(hidden).astype(jnp.bfloat16)
    mixed_term = jnp.einsum(
        "brwh,hd->brwd", activated, down_weight, preferred_element_type=jnp.float32
    )
    output = (residual_vals + channel_share(mixed_term)).astype(jnp.bfloat16)
    grad_hidden = (grad_act * gelu_slope(hidden)).astype(jnp.bfloat16)
    grad_term = jnp.einsum(
        "brwh,dh->brwd", grad_hidden, up_weight, preferred_element_type=jnp.float32
    )
    total_one, total_two = token_sums(
        jnp.sum(grad_term, axis=-1), jnp.sum(grad_term * vhat, axis=-1)
    )
    grad_vhat = channel_share(grad_term)
    own_hat = (residual_vals - mean_two) * rstd_two
    grad_residual = cotangent.astype(jnp.float32) + rstd_two * (
        grad_vhat
        - total_one[..., None] / full_width
        - own_hat * (total_two[..., None] / full_width)
    )
    grad_spec = lat_stacked(
        lat_forward_op,
        stacked_columns(
            lon_stacked_forward(grad_residual, lon_inv_tables, lax.Precision.DEFAULT), jnp.bfloat16
        ),
        lax.Precision.DEFAULT,
    )
    grad_second = jnp.where(jnp.abs(second) > SHRINK_LEVEL, to_blocks(grad_spec, block_size), 0.0)
    grad_first = jnp.where(first > 0.0, block_stacked_adjoint(grad_second, second_op), 0.0)
    grad_spectrum = block_stacked_adjoint(grad_first, first_op).reshape(spec.shape)
    grad_normed = grad_residual + lon_stacked_back(
        stacked_rows(
            lat_stacked(lat_inverse_op, grad_spectrum, lax.Precision.DEFAULT), jnp.bfloat16
        ),
        lon_fwd_tables,
        lax.Precision.DEFAULT,
    )
    norm_one, norm_two = token_sums(
        jnp.sum(grad_normed, axis=-1), jnp.sum(grad_normed * normed, axis=-1)
    )
    grad_input = grad_residual + rstd_one * (
        grad_normed - norm_one[..., None] / full_width - normed * (norm_two[..., None] / full_width)
    )
    return (output, grad_input.astype(jnp.bfloat16))


def solution(mesh):
    return jax.shard_map(
        per_device,
        mesh=mesh,
        in_specs=(
            P(None, "space", None, "feat"),
            P(None, "space", None, "feat"),
            P(None, "feat", None, None),
            P(None, "feat"),
            P(None, "feat", None, None),
            P(None, "feat"),
            P(None, "feat"),
            P("feat", None),
        ),
        out_specs=(P(None, "space", None, "feat"), P(None, "space", None, "feat")),
        check_vma=False,
    )
```

profile of v0, /device:TPU:1, one launch (start us, length us, event | category | flops | bytes accessed | tf_op | source)
XLA Modules:
  0.0 219.6 jit_solution(13806531281613694137)
XLA Ops:
  7.2 1.7 convert_reduce_fusion.1
  9.0 3.8 %collective-permute-start.1 = (f32[2,2,3,180]{3,2,1,0:T(4,128)S(1)}, f32[2,2,3,180]{3,2,1,0:T(4,128)S(1)}, u32[]{:S(2)}, u32[]{:S(2)}) collective-permute-start(f32[2,2,3,180]{3,2,1,0:T(4,128)S(1)} %pad_maximum_fusion.8), channel_id=1, source_target_pairs={{0,2},{1,3},{2,0},{3,1},{4,6},{5,7},{6,4},{7,5},{8,10},{9,11},{10,... | collective-permute-start | bytes 25928 | tf_op jit(solution)/shard_map/ppermute | solution.py:163
  13.2 2.3 %collective-permute-start = (f32[2,2,3,180]{3,2,1,0:T(4,128)S(1)}, f32[2,2,3,180]{3,2,1,0:T(4,128)S(1)}, u32[]{:S(2)}, u32[]{:S(2)}) collective-permute-start(f32[2,2,3,180]{3,2,1,0:T(4,128)S(1)} %pad_maximum_fusion.8), channel_id=1, source_target_pairs={{0,3},{1,0},{2,1},{3,2},{4,7},{5,4},{6,5},{7,6},{8,11},{9,8},{10,9... | collective-permute-start | bytes 25928 | tf_op jit(solution)/shard_map/ppermute | solution.py:163
  16.8 0.4 fusion.97
  17.4 0.7 pad_maximum_fusion.1
  18.2 1.1 maximum_bitcast_fusion.1
  19.3 0.7 pad_maximum_fusion.3
  20.1 1.0 convolution_bitcast_fusion.7
  21.1 0.9 copy.96
  22.0 28.2 %all_to_all.72 = f32[2,2,3,96,256]{4,1,2,0,3:T(2,128)S(1)} all-to-all(f32[2,2,3,96,256]{4,1,2,0,3:T(2,128)S(1)} %copy.96), channel_id=1, replica_groups=mesh['space'=32,'feat'=4] {'space'}, dimensions={3} | all-to-all | bytes 2359296 | tf_op jit(solution)/shard_map/all_to_all | solution.py:150
  50.6 0.7 convolution_bitcast_fusion.6
  51.3 1.6 reshape.195
  52.9 2.1 fusion.31
  55.1 0.7 fusion.32
  55.7 1.0 copy-done.1
  56.8 1.0 copy_bitcast_fusion
  57.7 1.4 fusion.42
  59.1 0.6 copy.108
  59.8 16.0 %all_to_all.73 = bf16[2,2,96,3,256]{4,0,3,1,2:T(2,128)(2,1)S(1)} all-to-all(bf16[2,2,96,3,256]{4,0,3,1,2:T(2,128)(2,1)S(1)} %copy.108), channel_id=1, replica_groups=mesh['space'=32,'feat'=4] {'space'}, dimensions={2} | all-to-all | bytes 1179648 | tf_op jit(solution)/shard_map/all_to_all | solution.py:154
  75.8 0.5 copy.110
  76.2 1.3 fusion.37
  77.6 6.9 %fusion.16 = f32[2,3,180,1024]{3,2,1,0:T(8,128)} fusion(bf16[2,3,180,1024]{3,0,2,1:T(2,128)(2,1)} %all-gather.3.cloned.1.call-done, bf16[1024,1024]{1,0:T(8,128)(2,1)} %param.15), kind=kOutput, calls=%fused_computation.20 | convolution fusion | flops 2264924160 | bytes 8732672 | tf_op jit(solution)/shard_map/brwd,hd->brwh/dot_general | solution.py:251
  84.5 23.0 %all-gather.5.cloned.1.call-done = bf16[2,3,180,1024]{3,2,1,0:T(8,128)(2,1)} async-done(((bf16[2,3,180,256]{3,2,1,0:T(8,128)(2,1)}), bf16[2,3,180,1024]{3,2,1,0:T(8,128)(2,1)}) %all-gather.5.cloned.1.call-update) | async-done | bytes 2211856 | tf_op jit(solution)/shard_map/all_gather | solution.py:250
  107.6 2.5 %convert_reduce_fusion = (f32[2,3,180]{2,1,0:T(4,128)S(1)}, f32[2,3,180]{2,1,0:T(4,128)S(1)}) fusion(bf16[2,3,180,1024]{3,2,1,0:T(8,128)(2,1)} %all-gather.5.cloned.1.call-done), kind=kLoop, calls=%fused_computation.3 | loop fusion | flops 4421520 | bytes 2220480 | tf_op jit(solution)/shard_map/reduce_sum | solution.py:256
  110.2 2.8 %fusion.14 = f32[2,3,180,1024]{3,2,1,0:T(8,128)S(1)} fusion(bf16[2,3,180,1024]{3,2,1,0:T(8,128)(2,1)S(1)} %copy-done.8, f32[2,3,180]{2,1,0:T(4,128)S(1)} %get-tuple-element.60, f32[2,3,180]{2,1,0:T(4,128)S(1)} %get-tuple-element.59, bf16[1024,1024]{1,0:T(8,128)(2,1)S(1)} %copy-done), kind=kOutput, calls=%fused_computation.19 | convolution fusion | flops 2269347840 | bytes 8741312 | tf_op jit(solution)/shard_map/brwd,dh->brwh/dot_general | solution.py:260
  113.1 5.4 %fusion.123 = (f32[2,3,180]{2,1,0:T(4,128)S(1)}, f32[2,3,180]{2,1,0:T(4,128)S(1)}, bf16[2,3,180,1024]{3,2,1,0:T(8,128)(2,1)}) fusion(f32[2,3,180]{2,1,0:T(4,128)S(1)} %get-tuple-element.60, f32[2,3,180]{2,1,0:T(4,128)S(1)} %get-tuple-element.59, bf16[2,3,180,1024]{3,2,1,0:T(8,128)(2,1)S(1)} %copy-done.8, bf16[1024,1024]{1,0:T(8,128)(2,1)S(1)} %copy-done, ...), kind=kOutput, calls=%fused_computation.189 | convolution fusion | flops 2283722752 | bytes 15385472 | tf_op jit(solution)/shard_map/brwh,dh->brwd/dot_general | solution.py:269
  118.5 6.9 %fusion.28 = bf16[2,3,180,1024]{3,2,1,0:T(8,128)(2,1)} fusion(bf16[1024,1024]{1,0:T(8,128)(2,1)} %param.15, f32[2,3,180,1024]{3,2,1,0:T(8,128)} %copy-done.19), kind=kOutput, calls=%fused_computation.36 | convolution fusion | flops 2271559680 | bytes 8732672 | tf_op jit(solution)/shard_map/brwh,hd->brwd/dot_general | solution.py:264
  125.5 2.5 %collective-permute-start.4 = (f32[2,2,3,180]{3,2,1,0:T(4,128)S(1)}, f32[2,2,3,180]{3,2,1,0:T(4,128)S(1)}, u32[]{:S(2)}, u32[]{:S(2)}) collective-permute-start(f32[2,2,3,180]{3,2,1,0:T(4,128)S(1)} %pad_maximum_fusion.9), channel_id=1, source_target_pairs={{0,2},{1,3},{2,0},{3,1},{4,6},{5,7},{6,4},{7,5},{8,10},{9,11},{10,... | collective-permute-start | bytes 25928 | tf_op jit(solution)/shard_map/ppermute | solution.py:163
  128.0 2.7 %collective-permute-start.3 = (f32[2,2,3,180]{3,2,1,0:T(4,128)S(1)}, f32[2,2,3,180]{3,2,1,0:T(4,128)S(1)}, u32[]{:S(2)}, u32[]{:S(2)}) collective-permute-start(f32[2,2,3,180]{3,2,1,0:T(4,128)S(1)} %pad_maximum_fusion.9), channel_id=1, source_target_pairs={{0,3},{1,0},{2,1},{3,2},{4,7},{5,4},{6,5},{7,6},{8,11},{9,8},{10,9... | collective-permute-start | bytes 25928 | tf_op jit(solution)/shard_map/ppermute | solution.py:163
  130.7 1.3 collective-permute-done.5
  132.0 19.8 %reduce-scatter.5.cloned.1.call-done = bf16[2,3,180,256]{3,2,1,0:T(8,128)(2,1)} async-done(((bf16[2,3,180,1024]{3,2,1,0:T(8,128)(2,1)}), bf16[2,3,180,256]{3,2,1,0:T(8,128)(2,1)}) %reduce-scatter.5.cloned.1.call-update) | async-done | bytes 552976 | tf_op jit(solution)/shard_map/reduce_scatter | solution.py:194
  151.8 2.3 %fusion.40 = bf16[2,2,3,96,256]{4,3,2,1,0:T(8,128)(2,1)S(1)} fusion(bf16[2,180,96]{2,1,0:T(8,128)(2,1)} %pad_maximum_fusion.3, bf16[2,3,180,256]{3,2,1,0:T(8,128)(2,1)} %fusion.37, bf16[2,3,180,256]{3,2,1,0:T(8,128)(2,1)} %reduce-scatter.5.cloned.1.call-done, bf16[2,3,180,256]{3,0,2,1:T(2,128)(2,1)} %param.9, f32[2,3,180]{2,1,0:T(4,128)S(1)} %get-tuple-element.58, ...), kind=kOutput, calls=%fused_computation.61 | convolution fusion | flops 108933120 | bytes 2335104 | tf_op jit(solution)/shard_map/brwc,pwk->pbrkc/dot_general | solution.py:130
  154.1 0.6 copy.114
  154.7 19.7 %all_to_all.74 = bf16[2,2,3,96,256]{4,1,2,0,3:T(2,128)(2,1)S(1)} all-to-all(bf16[2,2,3,96,256]{4,1,2,0,3:T(2,128)(2,1)S(1)} %copy.114), channel_id=1, replica_groups=mesh['space'=32,'feat'=4] {'space'}, dimensions={3} | all-to-all | bytes 1179648 | tf_op jit(solution)/shard_map/all_to_all | solution.py:150
  174.8 1.2 convolution_bitcast_fusion.8
  176.0 2.5 %reshape.229 = bf16[2,2,96,3,2,128]{5,4,2,0,3,1:T(2,128)(2,1)} reshape(bf16[2,2,96,3,256]{4,2,0,3,1:T(8,128)(2,1)} %convolution_bitcast_fusion.8) | data formatting | bytes 1179648 | tf_op jit(solution)/shard_map/reshape | solution.py:60
  178.5 2.1 fusion.39
  181.0 0.6 copy.189
  182.3 0.6 copy.126
  183.0 15.9 %all_to_all.75 = bf16[2,2,96,3,256]{4,0,3,1,2:T(2,128)(2,1)S(1)} all-to-all(bf16[2,2,96,3,256]{4,0,3,1,2:T(2,128)(2,1)S(1)} %copy.126), channel_id=1, replica_groups=mesh['space'=32,'feat'=4] {'space'}, dimensions={2} | all-to-all | bytes 1179648 | tf_op jit(solution)/shard_map/all_to_all | solution.py:154
  198.9 0.5 copy.128
  199.4 2.7 %fusion.124 = (f32[2,3,180]{2,1,0:T(4,128)S(1)}, f32[2,3,180]{2,1,0:T(4,128)S(1)}, f32[2,3,180,256]{3,2,1,0:T(8,128)}) fusion(f32[2,3,180]{2,1,0:T(4,128)S(1)} %fusion.115, f32[2,3,180]{2,1,0:T(4,128)S(1)} %fusion.116, bf16[2,3,180,256]{3,0,2,1:T(2,128)(2,1)S(1)} %copy-done.4, bf16[2,2,3,96,256]{4,1,3,2,0:T(2,128)(2,1)S(1)} %bitcast.284, ...), kind=kOutput, calls=%fused_computation.190 | convolution fusion | flops 110866320 | bytes 4080384 | tf_op jit(solution)/shard_map/pbrkc,pwk->brwc/dot_general | solution.py:134
  202.1 1.3 collective-permute-start.7
  203.4 2.6 %collective-permute-start.6 = (f32[2,2,3,180]{3,2,1,0:T(4,128)S(1)}, f32[2,2,3,180]{3,2,1,0:T(4,128)S(1)}, u32[]{:S(2)}, u32[]{:S(2)}) collective-permute-start(f32[2,2,3,180]{3,2,1,0:T(4,128)S(1)} %pad_maximum_fusion.10), channel_id=1, source_target_pairs={{0,3},{1,0},{2,1},{3,2},{4,7},{5,4},{6,5},{7,6},{8,11},{9,8},{10,9... | collective-permute-start | bytes 25928 | tf_op jit(solution)/shard_map/ppermute | solution.py:163
  206.3 0.9 collective-permute-done.8
  207.3 3.4 %fusion.68 = (bf16[2,3,180,256]{3,2,1,0:T(8,128)(2,1)S(1)}, bf16[2,3,180,256]{3,2,1,0:T(8,128)(2,1)S(1)}) fusion(f32[2,3,180,256]{3,2,1,0:T(8,128)} %get-tuple-element.64, f32[2,3,180]{2,1,0:T(4,128)S(1)} %get-tuple-element.56, f32[2,3,180]{2,1,0:T(4,128)S(1)} %get-tuple-element.55, f32[2,3,180]{2,1,0:T(4,128)S(1)} %fusion.115, ...), kind=kLoop, calls=%fused_computation.92 | loop fusion | flops 6082560 | bytes 5011200 | tf_op jit(solution)/shard_map/convert_element_type | solution.py:305
  210.6 1.2 copy.131
  211.9 1.2 copy.130
  (95 shorter events, 4.5 us)
Async XLA Ops:
  7.2 103.0 %copy-start = (bf16[1024,1024]{1,0:T(8,128)(2,1)S(1)}, bf16[1024,1024]{1,0:T(8,128)(2,1)}, u32[]{:S(2)}) copy-start(bf16[1024,1024]{1,0:T(8,128)(2,1)} %param.14) | copy-start | bytes 6291460
  7.2 10.1 %copy-start.14 = (f32[2,2,128,128]{3,2,1,0:T(8,128)S(1)}, f32[2,2,128,128]{3,2,1,0:T(8,128)}, u32[]{:S(2)}) copy-start(f32[2,2,128,128]{3,2,1,0:T(8,128)} %param.10) | copy-start | bytes 786436
  7.2 50.5 %all-gather.3.cloned.1.call-start = ((), (), s32[]{:S(2)}) async-start(), calls=%async_computation.6 | async-start | bytes 2764800 | tf_op jit(solution)/shard_map/all_gather | solution.py:227
  9.0 8.4 %copy-start.15 = (f32[2,2,128,128]{3,2,1,0:T(8,128)S(1)}, f32[2,2,128,128]{3,2,1,0:T(8,128)}, u32[]{:S(2)}) copy-start(f32[2,2,128,128]{3,2,1,0:T(8,128)} %param.12) | copy-start | bytes 786436
  9.0 11.0 %collective-permute-start.1 = (f32[2,2,3,180]{3,2,1,0:T(4,128)S(1)}, f32[2,2,3,180]{3,2,1,0:T(4,128)S(1)}, u32[]{:S(2)}, u32[]{:S(2)}) collective-permute-start(f32[2,2,3,180]{3,2,1,0:T(4,128)S(1)} %pad_maximum_fusion.8), channel_id=1, source_target_pairs={{0,2},{1,3},{2,0},{3,1},{4,6},{5,7},{6,4},{7,5},{8,10},{9,11},{10,... | collective-permute-start | bytes 25928 | tf_op jit(solution)/shard_map/ppermute | solution.py:163
  12.8 7.2 %collective-permute-start.2 = (f32[2,2,3,180]{3,2,1,0:T(4,128)S(1)}, f32[2,2,3,180]{3,2,1,0:T(4,128)S(1)}, u32[]{:S(2)}, u32[]{:S(2)}) collective-permute-start(f32[2,2,3,180]{3,2,1,0:T(4,128)S(1)} %pad_maximum_fusion.8), channel_id=1, source_target_pairs={{0,1},{1,2},{2,3},{3,0},{4,5},{5,6},{6,7},{7,4},{8,9},{9,10},{10,1... | collective-permute-start | bytes 25928 | tf_op jit(solution)/shard_map/ppermute | solution.py:163
  13.2 6.8 %collective-permute-start = (f32[2,2,3,180]{3,2,1,0:T(4,128)S(1)}, f32[2,2,3,180]{3,2,1,0:T(4,128)S(1)}, u32[]{:S(2)}, u32[]{:S(2)}) collective-permute-start(f32[2,2,3,180]{3,2,1,0:T(4,128)S(1)} %pad_maximum_fusion.8), channel_id=1, source_target_pairs={{0,3},{1,0},{2,1},{3,2},{4,7},{5,4},{6,5},{7,6},{8,11},{9,8},{10,9... | collective-permute-start | bytes 25928 | tf_op jit(solution)/shard_map/ppermute | solution.py:163
  15.5 92.1 %all-gather.5.cloned.1.call-start = ((), (), s32[]{:S(2)}) async-start(), calls=%async_computation.7 | async-start | bytes 2826240 | tf_op jit(solution)/shard_map/all_gather | solution.py:250
  17.4 2.6 %copy-start.11 = (f32[2,180,96]{2,1,0:T(8,128)}, f32[2,180,96]{2,1,0:T(8,128)S(1)}, u32[]{:S(2)}) copy-start(f32[2,180,96]{2,1,0:T(8,128)S(1)} %pad_maximum_fusion.2) | copy-start | bytes 414724
  18.2 1.8 copy-start.2
  51.3 1.6 copy-start.17
  52.9 2.1 copy-start.6
  52.9 2.1 copy-start.18
  55.7 1.0 copy-start.1
  59.8 16.5 %copy-start.3 = (bf16[2,3,180,256]{3,0,2,1:T(2,128)(2,1)S(1)}, bf16[2,3,180,256]{3,0,2,1:T(2,128)(2,1)}, u32[]{:S(2)}) copy-start(bf16[2,3,180,256]{3,0,2,1:T(2,128)(2,1)} %param.8) | copy-start | bytes 1658884
  59.8 16.5 %copy-start.16 = (bf16[2,180,96]{2,1,0:T(8,128)(2,1)S(1)}, bf16[2,180,96]{2,1,0:T(8,128)(2,1)}, u32[]{:S(2)}) copy-start(bf16[2,180,96]{2,1,0:T(8,128)(2,1)} %pad_maximum_fusion.3) | copy-start | bytes 207364
  77.6 74.2 %reduce-scatter.5.cloned.1.call-start = ((), (), s32[]{:S(2)}) async-start(), calls=%async_computation.9 | async-start | bytes 2826240 | tf_op jit(solution)/shard_map/reduce_scatter | solution.py:194
  107.6 2.6 %copy-start.8 = (bf16[2,3,180,1024]{3,2,1,0:T(8,128)(2,1)S(1)}, bf16[2,3,180,1024]{3,2,1,0:T(8,128)(2,1)}, u32[]{:S(2)}) copy-start(bf16[2,3,180,1024]{3,2,1,0:T(8,128)(2,1)} %all-gather.5.cloned.1.call-done) | copy-start | bytes 6635524
  107.6 5.4 %slice-start = ((s8[4521984]{0:T(1024)(128)(4,1)}), s8[4194304]{0:T(1024)(128)(4,1)S(1)}, s32[]{:S(2)}) async-start(s8[4521984]{0:T(1024)(128)(4,1)} %bitcast.300), calls=%async_computation.10 | async-start | bytes 8388608
  110.2 2.9 %slice-start.1 = ((s8[4521984]{0:T(1024)(128)(4,1)}), s8[327680]{0:T(1024)(128)(4,1)S(1)}, s32[]{:S(2)}) async-start(s8[4521984]{0:T(1024)(128)(4,1)} %bitcast.300), calls=%async_computation.11 | async-start | bytes 655360
  113.0 5.4 %copy-start.19 = (f32[2,3,180,1024]{3,2,1,0:T(8,128)}, f32[2,3,180,1024]{3,2,1,0:T(8,128)S(1)}, u32[]{:S(2)}) copy-start(f32[2,3,180,1024]{3,2,1,0:T(8,128)S(1)} %fusion.14) | copy-start | bytes 13271044
  118.5 88.8 %reduce-scatter.3.cloned.1.call-start = ((), (), s32[]{:S(2)}) async-start(), calls=%async_computation.8 | async-start | bytes 2826240 | tf_op jit(solution)/shard_map/reduce_scatter | solution.py:194
  125.5 5.2 %collective-permute-start.4 = (f32[2,2,3,180]{3,2,1,0:T(4,128)S(1)}, f32[2,2,3,180]{3,2,1,0:T(4,128)S(1)}, u32[]{:S(2)}, u32[]{:S(2)}) collective-permute-start(f32[2,2,3,180]{3,2,1,0:T(4,128)S(1)} %pad_maximum_fusion.9), channel_id=1, source_target_pairs={{0,2},{1,3},{2,0},{3,1},{4,6},{5,7},{6,4},{7,5},{8,10},{9,11},{10,... | collective-permute-start | bytes 25928 | tf_op jit(solution)/shard_map/ppermute | solution.py:163
  128.0 4.0 %collective-permute-start.5 = (f32[2,2,3,180]{3,2,1,0:T(4,128)S(1)}, f32[2,2,3,180]{3,2,1,0:T(4,128)S(1)}, u32[]{:S(2)}, u32[]{:S(2)}) collective-permute-start(f32[2,2,3,180]{3,2,1,0:T(4,128)S(1)} %pad_maximum_fusion.9), channel_id=1, source_target_pairs={{0,1},{1,2},{2,3},{3,0},{4,5},{5,6},{6,7},{7,4},{8,9},{9,10},{10,1... | collective-permute-start | bytes 25928 | tf_op jit(solution)/shard_map/ppermute | solution.py:163
  128.0 4.0 %collective-permute-start.3 = (f32[2,2,3,180]{3,2,1,0:T(4,128)S(1)}, f32[2,2,3,180]{3,2,1,0:T(4,128)S(1)}, u32[]{:S(2)}, u32[]{:S(2)}) collective-permute-start(f32[2,2,3,180]{3,2,1,0:T(4,128)S(1)} %pad_maximum_fusion.9), channel_id=1, source_target_pairs={{0,3},{1,0},{2,1},{3,2},{4,7},{5,4},{6,5},{7,6},{8,11},{9,8},{10,9... | collective-permute-start | bytes 25928 | tf_op jit(solution)/shard_map/ppermute | solution.py:163
  178.5 2.1 copy-start.5
  180.9 1.0 copy-start.10
  182.3 17.0 %copy-start.13 = (bf16[2,3,180,256]{3,2,1,0:T(8,128)(2,1)S(1)}, bf16[2,3,180,256]{3,2,1,0:T(8,128)(2,1)}, u32[]{:S(2)}) copy-start(bf16[2,3,180,256]{3,2,1,0:T(8,128)(2,1)} %reduce-scatter.5.cloned.1.call-done) | copy-start | bytes 1658884
  183.0 16.4 %copy-start.4 = (bf16[2,3,180,256]{3,0,2,1:T(2,128)(2,1)S(1)}, bf16[2,3,180,256]{3,0,2,1:T(2,128)(2,1)}, u32[]{:S(2)}) copy-start(bf16[2,3,180,256]{3,0,2,1:T(2,128)(2,1)} %param.8) | copy-start | bytes 1658884
  183.0 16.4 %copy-start.7 = (bf16[2,3,180,256]{3,2,1,0:T(8,128)(2,1)S(1)}, bf16[2,3,180,256]{3,2,1,0:T(8,128)(2,1)}, u32[]{:S(2)}) copy-start(bf16[2,3,180,256]{3,2,1,0:T(8,128)(2,1)} %fusion.37) | copy-start | bytes 1658884
  183.0 16.4 %copy-start.9 = (bf16[2,3,180,256]{3,0,2,1:T(2,128)(2,1)S(1)}, bf16[2,3,180,256]{3,0,2,1:T(2,128)(2,1)}, u32[]{:S(2)}) copy-start(bf16[2,3,180,256]{3,0,2,1:T(2,128)(2,1)} %param.9) | copy-start | bytes 1658884
  183.0 16.4 %copy-start.12 = (f32[2,180,96]{2,1,0:T(8,128)S(1)}, f32[2,180,96]{2,1,0:T(8,128)}, u32[]{:S(2)}) copy-start(f32[2,180,96]{2,1,0:T(8,128)} %copy-done.11) | copy-start | bytes 414724
  202.1 4.2 %collective-permute-start.7 = (f32[2,2,3,180]{3,2,1,0:T(4,128)S(1)}, f32[2,2,3,180]{3,2,1,0:T(4,128)S(1)}, u32[]{:S(2)}, u32[]{:S(2)}) collective-permute-start(f32[2,2,3,180]{3,2,1,0:T(4,128)S(1)} %pad_maximum_fusion.10), channel_id=1, source_target_pairs={{0,2},{1,3},{2,0},{3,1},{4,6},{5,7},{6,4},{7,5},{8,10},{9,11},{10,... | collective-permute-start | bytes 25928 | tf_op jit(solution)/shard_map/ppermute | solution.py:163
  203.4 3.8 %collective-permute-start.8 = (f32[2,2,3,180]{3,2,1,0:T(4,128)S(1)}, f32[2,2,3,180]{3,2,1,0:T(4,128)S(1)}, u32[]{:S(2)}, u32[]{:S(2)}) collective-permute-start(f32[2,2,3,180]{3,2,1,0:T(4,128)S(1)} %pad_maximum_fusion.10), channel_id=1, source_target_pairs={{0,1},{1,2},{2,3},{3,0},{4,5},{5,6},{6,7},{7,4},{8,9},{9,10},{10,1... | collective-permute-start | bytes 25928 | tf_op jit(solution)/shard_map/ppermute | solution.py:163
  203.4 3.8 %collective-permute-start.6 = (f32[2,2,3,180]{3,2,1,0:T(4,128)S(1)}, f32[2,2,3,180]{3,2,1,0:T(4,128)S(1)}, u32[]{:S(2)}, u32[]{:S(2)}) collective-permute-start(f32[2,2,3,180]{3,2,1,0:T(4,128)S(1)} %pad_maximum_fusion.10), channel_id=1, source_target_pairs={{0,3},{1,0},{2,1},{3,2},{4,7},{5,4},{6,5},{7,6},{8,11},{9,8},{10,9... | collective-permute-start | bytes 25928 | tf_op jit(solution)/shard_map/ppermute | solution.py:163
Sparse Core Ops, SparseCore 0:
  15.6 35.1 all-gather.2
  77.7 29.8 all-gather.4
  118.6 33.1 reduce-scatter.4
  154.2 30.7 reduce-scatter.2
where the time goes:
time: 220 us
  blocking collectives  79.8 us (36%)
  waiting for transfers between devices  45.3 us (21%)
  matrix products  38.3 us (17%)
  starting transfers between devices  15.8 us (7%)
  between operations  14.4 us (7%)
  local copies, waits for them, and re-layouts  13.1 us (6%)
  other arithmetic  12.9 us (6%)
    all_to_all x2, blocking collectives, stacked_columns(): lax.all_to_all(field.astype(link_type), 'space', 3, 2, tiled=True)  47.9 us
    all_to_all x2, blocking collectives, stacked_rows(): lax.all_to_all(field.astype(link_type), 'space', 2, 3, tiled=True)  31.9 us
    all_gather x1, waiting for transfers between devices, per_device(): whole_residual = lax.all_gather(residual, 'feat', axis=3, tiled=True)  23 us
    reduce_scatter x2, waiting for transfers between devices, channel_share(): lax.psum_scatter(term.astype(jnp.bfloat16), 'feat', scatter_dimension=3,...  19.8 us
    ppermute x9, starting transfers between devices, token_sums(): lax.ppermute(pair, 'feat', [(i, (i + count - shift) % count) for i in ran...  15.6 us
    dot_general x1, matrix products, per_device(): jnp.einsum('brwd,hd->brwh', whole_cotangent, down_weight, preferred_eleme...  6.92 us
    dot_general x1, matrix products, per_device(): jnp.einsum('brwh,hd->brwd', activated, down_weight, preferred_element_typ...  6.91 us
    dot_general x1, matrix products, per_device(): jnp.einsum('brwh,dh->brwd', grad_hidden, up_weight, preferred_element_typ...  5.41 us
  transfers between devices with their start and end apart: 13, of which 5 were waited for; matrix products, arithmetic and copies ran while one was open for 19% of the time, Pallas kernels for 0%

commit v1 on v0

--- a/solution.py
+++ b/solution.py
@@ -151,7 +151,15 @@
 
 
 def stacked_rows(field, link_type):
-    return lax.all_to_all(field.astype(link_type), "space", 2, 3, tiled=True).astype(jnp.float32)
+    return jnp.concatenate(
+        lax.all_to_all(
+            jnp.stack(jnp.split(field.astype(link_type), lax.axis_size("space"), axis=2)),
+            "space",
+            0,
+            0,
+        ),
+        axis=3,
+    ).astype(jnp.float32)
 
 
 def token_sums(first_term, second_term):

time: 220 us -> 224 us (1.018)
  blocking collectives: 79.8 us -> 59.9 us
  waiting for transfers between devices: 45.3 us -> 57.2 us
  starting transfers between devices: 15.8 us -> 23.6 us
  local copies, waits for them, and re-layouts: 13.1 us -> 16.4 us
    all_to_all x2 -> x1, blocking collectives: 47.9 us -> 28.2 us  [stacked_columns(): lax.all_to_all(field.astype(link_type), 'space', 3, 2, tiled=True)]
    all_to_all x0 -> x1, starting transfers between devices: none -> 7.66 us  [stacked_columns(): lax.all_to_all(field.astype(link_type), 'space', 3, 2, tiled=True)]
    reduce_scatter x2, waiting for transfers between devices: 19.8 us -> 26.6 us  [channel_share(): lax.psum_scatter(term.astype(jnp.bfloat16), 'feat', scatter_dimension=3,...]
    all_to_all x0 -> x1, waiting for transfers between devices: none -> 5.13 us  [stacked_columns(): lax.all_to_all(field.astype(link_type), 'space', 3, 2, tiled=True)]
    unnamed x46 -> x108, local copies, waits for them, and re-layouts: 3.58 us -> 5.02 us
  transfers between devices with their start and end apart: 13 -> 14, of which waited for: 5 -> 6; matrix products, arithmetic and copies ran while one was open for 19% -> 18% of each run, Pallas kernels for 0% -> 0%
where the time goes in v1:
time: 224 us; the launch traced here: 223 us
  blocking collectives  59.9 us (27%)
  waiting for transfers between devices  57.2 us (26%)
  matrix products  38.3 us (17%)
  starting transfers between devices  23.6 us (11%)
  local copies, waits for them, and re-layouts  16.4 us (7%)
  between operations  14.7 us (7%)
  other arithmetic  12.9 us (6%)
    all_to_all x2, blocking collectives, stacked_rows(): lax.all_to_all(jnp.stack(jnp.split(field.astype(link_type), lax.axis_size...  31.8 us
    all_to_all x1, blocking collectives, stacked_columns(): lax.all_to_all(field.astype(link_type), 'space', 3, 2, tiled=True)  28.2 us
    reduce_scatter x2, waiting for transfers between devices, channel_share(): lax.psum_scatter(term.astype(jnp.bfloat16), 'feat', scatter_dimension=3,...  26.6 us
    all_gather x1, waiting for transfers between devices, per_device(): whole_residual = lax.all_gather(residual, 'feat', axis=3, tiled=True)  23.1 us
    ppermute x9, starting transfers between devices, token_sums(): lax.ppermute(pair, 'feat', [(i, (i + count - shift) % count) for i in ran...  15.6 us
    all_to_all x1, starting transfers between devices, stacked_columns(): lax.all_to_all(field.astype(link_type), 'space', 3, 2, tiled=True)  7.66 us
    dot_general x1, matrix products, per_device(): jnp.einsum('brwh,hd->brwd', activated, down_weight, preferred_element_typ...  6.91 us
    dot_general x1, matrix products, per_device(): jnp.einsum('brwd,hd->brwh', whole_cotangent, down_weight, preferred_eleme...  6.91 us
  transfers between devices with their start and end apart: 14, of which 6 were waited for; matrix products, arithmetic and copies ran while one was open for 18% of the time, Pallas kernels for 0%

profile of v1, /device:TPU:1, one launch (start us, length us, event | category | flops | bytes accessed | tf_op | source)
XLA Modules:
  0.0 223.2 jit_solution(12978386506528940776)
XLA Ops:
  7.2 1.7 convert_reduce_fusion.1
  9.0 3.8 %collective-permute-start.1 = (f32[2,2,3,180]{3,2,1,0:T(4,128)S(1)}, f32[2,2,3,180]{3,2,1,0:T(4,128)S(1)}, u32[]{:S(2)}, u32[]{:S(2)}) collective-permute-start(f32[2,2,3,180]{3,2,1,0:T(4,128)S(1)} %pad_maximum_fusion.8), channel_id=1, source_target_pairs={{0,2},{1,3},{2,0},{3,1},{4,6},{5,7},{6,4},{7,5},{8,10},{9,11},{10,... | collective-permute-start | bytes 25928 | tf_op jit(solution)/shard_map/ppermute | solution.py:171
  13.2 2.3 %collective-permute-start = (f32[2,2,3,180]{3,2,1,0:T(4,128)S(1)}, f32[2,2,3,180]{3,2,1,0:T(4,128)S(1)}, u32[]{:S(2)}, u32[]{:S(2)}) collective-permute-start(f32[2,2,3,180]{3,2,1,0:T(4,128)S(1)} %pad_maximum_fusion.8), channel_id=1, source_target_pairs={{0,3},{1,0},{2,1},{3,2},{4,7},{5,4},{6,5},{7,6},{8,11},{9,8},{10,9... | collective-permute-start | bytes 25928 | tf_op jit(solution)/shard_map/ppermute | solution.py:171
  16.8 0.4 fusion.97
  17.4 0.7 pad_maximum_fusion.1
  18.2 1.1 maximum_bitcast_fusion.1
  19.3 0.7 pad_maximum_fusion.3
  20.1 1.0 convolution_bitcast_fusion.7
  21.1 0.9 copy.90
  22.0 28.2 %all_to_all.46 = f32[2,2,3,96,256]{4,1,2,0,3:T(2,128)S(1)} all-to-all(f32[2,2,3,96,256]{4,1,2,0,3:T(2,128)S(1)} %copy.90), channel_id=1, replica_groups=mesh['space'=32,'feat'=4] {'space'}, dimensions={3} | all-to-all | bytes 2359296 | tf_op jit(solution)/shard_map/all_to_all | solution.py:150
  50.6 0.7 convolution_bitcast_fusion.6
  51.3 1.6 reshape.207
  52.9 2.1 fusion.31
  55.1 0.7 fusion.32
  55.7 1.0 copy-done.1
  56.7 1.0 copy_bitcast_fusion
  57.7 1.4 fusion.42
  60.0 0.5 copy.102
  60.6 16.0 %all_to_all.47 = bf16[32,2,2,3,3,256]{5,2,4,3,1,0:T(2,128)(2,1)S(1)} all-to-all(bf16[32,2,2,3,3,256]{5,2,4,3,1,0:T(2,128)(2,1)S(1)} %copy.102), channel_id=1, replica_groups=mesh['space'=32,'feat'=4] {'space'}, dimensions={0} | all-to-all | bytes 1179648 | tf_op jit(solution)/shard_map/all_to_all | solution.py:155
  77.0 1.3 fusion.37
  78.4 6.9 %fusion.16 = f32[2,3,180,1024]{3,2,1,0:T(8,128)} fusion(bf16[2,3,180,1024]{3,0,2,1:T(2,128)(2,1)} %all-gather.3.cloned.1.call-done, bf16[1024,1024]{1,0:T(8,128)(2,1)} %param.15), kind=kOutput, calls=%fused_computation.20 | convolution fusion | flops 2264924160 | bytes 8732672 | tf_op jit(solution)/shard_map/brwd,hd->brwh/dot_general | solution.py:259
  85.3 23.1 %all-gather.5.cloned.1.call-done = bf16[2,3,180,1024]{3,2,1,0:T(8,128)(2,1)} async-done(((bf16[2,3,180,256]{3,2,1,0:T(8,128)(2,1)}), bf16[2,3,180,1024]{3,2,1,0:T(8,128)(2,1)}) %all-gather.5.cloned.1.call-update) | async-done | bytes 2211856 | tf_op jit(solution)/shard_map/all_gather | solution.py:258
  108.3 2.5 %convert_reduce_fusion = (f32[2,3,180]{2,1,0:T(4,128)S(1)}, f32[2,3,180]{2,1,0:T(4,128)S(1)}) fusion(bf16[2,3,180,1024]{3,2,1,0:T(8,128)(2,1)} %all-gather.5.cloned.1.call-done), kind=kLoop, calls=%fused_computation.3 | loop fusion | flops 4421520 | bytes 2220480 | tf_op jit(solution)/shard_map/reduce_sum | solution.py:264
  110.9 2.8 %fusion.14 = f32[2,3,180,1024]{3,2,1,0:T(8,128)S(1)} fusion(bf16[2,3,180,1024]{3,2,1,0:T(8,128)(2,1)S(1)} %copy-done.8, f32[2,3,180]{2,1,0:T(4,128)S(1)} %get-tuple-element.60, f32[2,3,180]{2,1,0:T(4,128)S(1)} %get-tuple-element.59, bf16[1024,1024]{1,0:T(8,128)(2,1)S(1)} %copy-done), kind=kOutput, calls=%fused_computation.19 | convolution fusion | flops 2269347840 | bytes 8741312 | tf_op jit(solution)/shard_map/brwd,dh->brwh/dot_general | solution.py:268
  113.8 5.4 %fusion.123 = (f32[2,3,180]{2,1,0:T(4,128)S(1)}, f32[2,3,180]{2,1,0:T(4,128)S(1)}, bf16[2,3,180,1024]{3,2,1,0:T(8,128)(2,1)}) fusion(f32[2,3,180]{2,1,0:T(4,128)S(1)} %get-tuple-element.60, f32[2,3,180]{2,1,0:T(4,128)S(1)} %get-tuple-element.59, bf16[2,3,180,1024]{3,2,1,0:T(8,128)(2,1)S(1)} %copy-done.8, bf16[1024,1024]{1,0:T(8,128)(2,1)S(1)} %copy-done, ...), kind=kOutput, calls=%fused_computation.317 | convolution fusion | flops 2283722752 | bytes 15385472 | tf_op jit(solution)/shard_map/brwh,dh->brwd/dot_general | solution.py:277
  119.3 2.5 %collective-permute-start.4 = (f32[2,2,3,180]{3,2,1,0:T(4,128)S(1)}, f32[2,2,3,180]{3,2,1,0:T(4,128)S(1)}, u32[]{:S(2)}, u32[]{:S(2)}) collective-permute-start(f32[2,2,3,180]{3,2,1,0:T(4,128)S(1)} %pad_maximum_fusion.9), channel_id=1, source_target_pairs={{0,2},{1,3},{2,0},{3,1},{4,6},{5,7},{6,4},{7,5},{8,10},{9,11},{10,... | collective-permute-start | bytes 25928 | tf_op jit(solution)/shard_map/ppermute | solution.py:171
  121.8 2.7 %collective-permute-start.3 = (f32[2,2,3,180]{3,2,1,0:T(4,128)S(1)}, f32[2,2,3,180]{3,2,1,0:T(4,128)S(1)}, u32[]{:S(2)}, u32[]{:S(2)}) collective-permute-start(f32[2,2,3,180]{3,2,1,0:T(4,128)S(1)} %pad_maximum_fusion.9), channel_id=1, source_target_pairs={{0,3},{1,0},{2,1},{3,2},{4,7},{5,4},{6,5},{7,6},{8,11},{9,8},{10,9... | collective-permute-start | bytes 25928 | tf_op jit(solution)/shard_map/ppermute | solution.py:171
  124.5 1.3 collective-permute-done.5
  125.8 26.6 %reduce-scatter.5.cloned.1.call-done = bf16[2,3,180,256]{3,2,1,0:T(8,128)(2,1)} async-done(((bf16[2,3,180,1024]{3,2,1,0:T(8,128)(2,1)}), bf16[2,3,180,256]{3,2,1,0:T(8,128)(2,1)}) %reduce-scatter.5.cloned.1.call-update) | async-done | bytes 552976 | tf_op jit(solution)/shard_map/reduce_scatter | solution.py:202
  152.3 2.3 %fusion.40 = bf16[2,2,3,96,256]{4,3,2,1,0:T(8,128)(2,1)S(1)} fusion(bf16[2,180,96]{2,1,0:T(8,128)(2,1)} %pad_maximum_fusion.3, bf16[2,3,180,256]{3,2,1,0:T(8,128)(2,1)} %fusion.37, bf16[2,3,180,256]{3,2,1,0:T(8,128)(2,1)} %reduce-scatter.5.cloned.1.call-done, bf16[2,3,180,256]{3,0,2,1:T(2,128)(2,1)} %param.9, f32[2,3,180]{2,1,0:T(4,128)S(1)} %get-tuple-element.58, ...), kind=kOutput, calls=%fused_computation.61 | convolution fusion | flops 108933120 | bytes 2335104 | tf_op jit(solution)/shard_map/brwc,pwk->pbrkc/dot_general | solution.py:130
  154.7 1.5 copy.107
  156.2 7.7 %all-to-all-start.2 = ((bf16[2,2,3,96,256]{4,1,2,0,3:T(2,128)(2,1)}), bf16[2,2,3,96,256]{4,1,2,0,3:T(2,128)(2,1)}, u32[]{:S(2)}, u32[]{:S(2)}) async-start(bf16[2,2,3,96,256]{4,1,2,0,3:T(2,128)(2,1)} %copy.107), calls=%async_computation.4 | async-start | bytes 1179648 | tf_op jit(solution)/shard_map/all_to_all | solution.py:150
  164.1 6.9 %fusion.28 = bf16[2,3,180,1024]{3,2,1,0:T(8,128)(2,1)} fusion(bf16[1024,1024]{1,0:T(8,128)(2,1)} %param.15, f32[2,3,180,1024]{3,2,1,0:T(8,128)} %copy-done.19), kind=kOutput, calls=%fused_computation.36 | convolution fusion | flops 2271559680 | bytes 8732672 | tf_op jit(solution)/shard_map/brwh,hd->brwd/dot_general | solution.py:272
  171.0 5.1 %all-to-all-done.2 = bf16[2,2,3,96,256]{4,1,2,0,3:T(2,128)(2,1)} async-done(((bf16[2,2,3,96,256]{4,1,2,0,3:T(2,128)(2,1)}), bf16[2,2,3,96,256]{4,1,2,0,3:T(2,128)(2,1)}, u32[]{:S(2)}, u32[]{:S(2)}) %all-to-all-start.2) | async-done | bytes 589856 | tf_op jit(solution)/shard_map/all_to_all | solution.py:150
  176.2 1.5 copy.109
  177.6 1.2 convolution_bitcast_fusion.8
  178.9 2.6 %reshape.245 = bf16[2,2,96,3,2,128]{5,4,2,0,3,1:T(2,128)(2,1)} reshape(bf16[2,2,96,3,256]{4,2,0,3,1:T(8,128)(2,1)} %convolution_bitcast_fusion.8) | data formatting | bytes 1179648 | tf_op jit(solution)/shard_map/reshape | solution.py:60
  181.5 2.1 fusion.39
  183.9 0.6 copy.180
  186.2 0.5 copy.119
  186.7 15.8 %all_to_all.48 = bf16[32,2,2,3,3,256]{5,2,4,3,1,0:T(2,128)(2,1)S(1)} all-to-all(bf16[32,2,2,3,3,256]{5,2,4,3,1,0:T(2,128)(2,1)S(1)} %copy.119), channel_id=1, replica_groups=mesh['space'=32,'feat'=4] {'space'}, dimensions={0} | all-to-all | bytes 1179648 | tf_op jit(solution)/shard_map/all_to_all | solution.py:155
  203.0 2.7 %fusion.124 = (f32[2,3,180]{2,1,0:T(4,128)S(1)}, f32[2,3,180]{2,1,0:T(4,128)S(1)}, f32[2,3,180,256]{3,2,1,0:T(8,128)}) fusion(f32[2,3,180]{2,1,0:T(4,128)S(1)} %fusion.115, f32[2,3,180]{2,1,0:T(4,128)S(1)} %fusion.116, bf16[2,3,180,256]{3,0,2,1:T(2,128)(2,1)S(1)} %copy-done.4, bf16[2,2,3,96,256]{4,1,3,2,0:T(2,128)(2,1)S(1)} %bitcast.535, ...), kind=kOutput, calls=%fused_computation.318 | convolution fusion | flops 110866320 | bytes 4080384 | tf_op jit(solution)/shard_map/pbrkc,pwk->brwc/dot_general | solution.py:134
  205.7 1.2 collective-permute-start.7
  206.9 2.7 %collective-permute-start.6 = (f32[2,2,3,180]{3,2,1,0:T(4,128)S(1)}, f32[2,2,3,180]{3,2,1,0:T(4,128)S(1)}, u32[]{:S(2)}, u32[]{:S(2)}) collective-permute-start(f32[2,2,3,180]{3,2,1,0:T(4,128)S(1)} %pad_maximum_fusion.10), channel_id=1, source_target_pairs={{0,3},{1,0},{2,1},{3,2},{4,7},{5,4},{6,5},{7,6},{8,11},{9,8},{10,9... | collective-permute-start | bytes 25928 | tf_op jit(solution)/shard_map/ppermute | solution.py:171
  209.9 0.9 collective-permute-done.8
  210.8 3.4 %fusion.68 = (bf16[2,3,180,256]{3,2,1,0:T(8,128)(2,1)S(1)}, bf16[2,3,180,256]{3,2,1,0:T(8,128)(2,1)S(1)}) fusion(f32[2,3,180,256]{3,2,1,0:T(8,128)} %get-tuple-element.64, f32[2,3,180]{2,1,0:T(4,128)S(1)} %get-tuple-element.56, f32[2,3,180]{2,1,0:T(4,128)S(1)} %get-tuple-element.55, f32[2,3,180]{2,1,0:T(4,128)S(1)} %fusion.115, ...), kind=kLoop, calls=%fused_computation.92 | loop fusion | flops 6082560 | bytes 5011200 | tf_op jit(solution)/shard_map/convert_element_type | solution.py:313
  214.2 1.2 copy.123
  215.4 1.2 copy.122
  (160 shorter events, 6.6 us)
Async XLA Ops:
  7.2 103.7 %copy-start = (bf16[1024,1024]{1,0:T(8,128)(2,1)S(1)}, bf16[1024,1024]{1,0:T(8,128)(2,1)}, u32[]{:S(2)}) copy-start(bf16[1024,1024]{1,0:T(8,128)(2,1)} %param.14) | copy-start | bytes 6291460
  7.2 10.1 %copy-start.14 = (f32[2,2,128,128]{3,2,1,0:T(8,128)S(1)}, f32[2,2,128,128]{3,2,1,0:T(8,128)}, u32[]{:S(2)}) copy-start(f32[2,2,128,128]{3,2,1,0:T(8,128)} %param.10) | copy-start | bytes 786436
  7.2 50.5 %all-gather.3.cloned.1.call-start = ((), (), s32[]{:S(2)}) async-start(), calls=%async_computation.6 | async-start | bytes 2764800 | tf_op jit(solution)/shard_map/all_gather | solution.py:235
  9.0 8.4 %copy-start.15 = (f32[2,2,128,128]{3,2,1,0:T(8,128)S(1)}, f32[2,2,128,128]{3,2,1,0:T(8,128)}, u32[]{:S(2)}) copy-start(f32[2,2,128,128]{3,2,1,0:T(8,128)} %param.12) | copy-start | bytes 786436
  9.0 11.0 %collective-permute-start.1 = (f32[2,2,3,180]{3,2,1,0:T(4,128)S(1)}, f32[2,2,3,180]{3,2,1,0:T(4,128)S(1)}, u32[]{:S(2)}, u32[]{:S(2)}) collective-permute-start(f32[2,2,3,180]{3,2,1,0:T(4,128)S(1)} %pad_maximum_fusion.8), channel_id=1, source_target_pairs={{0,2},{1,3},{2,0},{3,1},{4,6},{5,7},{6,4},{7,5},{8,10},{9,11},{10,... | collective-permute-start | bytes 25928 | tf_op jit(solution)/shard_map/ppermute | solution.py:171
  12.8 7.2 %collective-permute-start.2 = (f32[2,2,3,180]{3,2,1,0:T(4,128)S(1)}, f32[2,2,3,180]{3,2,1,0:T(4,128)S(1)}, u32[]{:S(2)}, u32[]{:S(2)}) collective-permute-start(f32[2,2,3,180]{3,2,1,0:T(4,128)S(1)} %pad_maximum_fusion.8), channel_id=1, source_target_pairs={{0,1},{1,2},{2,3},{3,0},{4,5},{5,6},{6,7},{7,4},{8,9},{9,10},{10,1... | collective-permute-start | bytes 25928 | tf_op jit(solution)/shard_map/ppermute | solution.py:171
  13.2 6.8 %collective-permute-start = (f32[2,2,3,180]{3,2,1,0:T(4,128)S(1)}, f32[2,2,3,180]{3,2,1,0:T(4,128)S(1)}, u32[]{:S(2)}, u32[]{:S(2)}) collective-permute-start(f32[2,2,3,180]{3,2,1,0:T(4,128)S(1)} %pad_maximum_fusion.8), channel_id=1, source_target_pairs={{0,3},{1,0},{2,1},{3,2},{4,7},{5,4},{6,5},{7,6},{8,11},{9,8},{10,9... | collective-permute-start | bytes 25928 | tf_op jit(solution)/shard_map/ppermute | solution.py:171
  15.5 92.8 %all-gather.5.cloned.1.call-start = ((), (), s32[]{:S(2)}) async-start(), calls=%async_computation.7 | async-start | bytes 2826240 | tf_op jit(solution)/shard_map/all_gather | solution.py:258
  17.4 2.7 %copy-start.11 = (f32[2,180,96]{2,1,0:T(8,128)}, f32[2,180,96]{2,1,0:T(8,128)S(1)}, u32[]{:S(2)}) copy-start(f32[2,180,96]{2,1,0:T(8,128)S(1)} %pad_maximum_fusion.2) | copy-start | bytes 414724
  18.2 1.8 copy-start.2
  51.3 1.6 copy-start.17
  52.9 2.1 copy-start.6
  52.9 2.1 copy-start.18
  55.7 1.0 copy-start.1
  60.5 16.4 %copy-start.3 = (bf16[2,3,180,256]{3,0,2,1:T(2,128)(2,1)S(1)}, bf16[2,3,180,256]{3,0,2,1:T(2,128)(2,1)}, u32[]{:S(2)}) copy-start(bf16[2,3,180,256]{3,0,2,1:T(2,128)(2,1)} %param.8) | copy-start | bytes 1658884
  60.6 16.4 %copy-start.16 = (bf16[2,180,96]{2,1,0:T(8,128)(2,1)S(1)}, bf16[2,180,96]{2,1,0:T(8,128)(2,1)}, u32[]{:S(2)}) copy-start(bf16[2,180,96]{2,1,0:T(8,128)(2,1)} %pad_maximum_fusion.3) | copy-start | bytes 207364
  78.3 74.0 %reduce-scatter.5.cloned.1.call-start = ((), (), s32[]{:S(2)}) async-start(), calls=%async_computation.9 | async-start | bytes 2826240 | tf_op jit(solution)/shard_map/reduce_scatter | solution.py:202
  108.3 2.6 %copy-start.8 = (bf16[2,3,180,1024]{3,2,1,0:T(8,128)(2,1)S(1)}, bf16[2,3,180,1024]{3,2,1,0:T(8,128)(2,1)}, u32[]{:S(2)}) copy-start(bf16[2,3,180,1024]{3,2,1,0:T(8,128)(2,1)} %all-gather.5.cloned.1.call-done) | copy-start | bytes 6635524
  108.3 5.4 %slice-start = ((s8[4521984]{0:T(1024)(128)(4,1)}), s8[4194304]{0:T(1024)(128)(4,1)S(1)}, s32[]{:S(2)}) async-start(s8[4521984]{0:T(1024)(128)(4,1)} %bitcast.551), calls=%async_computation.10 | async-start | bytes 8388608
  110.9 2.9 %slice-start.1 = ((s8[4521984]{0:T(1024)(128)(4,1)}), s8[327680]{0:T(1024)(128)(4,1)S(1)}, s32[]{:S(2)}) async-start(s8[4521984]{0:T(1024)(128)(4,1)} %bitcast.551), calls=%async_computation.11 | async-start | bytes 655360
  113.8 5.4 %copy-start.19 = (f32[2,3,180,1024]{3,2,1,0:T(8,128)}, f32[2,3,180,1024]{3,2,1,0:T(8,128)S(1)}, u32[]{:S(2)}) copy-start(f32[2,3,180,1024]{3,2,1,0:T(8,128)S(1)} %fusion.14) | copy-start | bytes 13271044
  119.3 5.2 %collective-permute-start.4 = (f32[2,2,3,180]{3,2,1,0:T(4,128)S(1)}, f32[2,2,3,180]{3,2,1,0:T(4,128)S(1)}, u32[]{:S(2)}, u32[]{:S(2)}) collective-permute-start(f32[2,2,3,180]{3,2,1,0:T(4,128)S(1)} %pad_maximum_fusion.9), channel_id=1, source_target_pairs={{0,2},{1,3},{2,0},{3,1},{4,6},{5,7},{6,4},{7,5},{8,10},{9,11},{10,... | collective-permute-start | bytes 25928 | tf_op jit(solution)/shard_map/ppermute | solution.py:171
  121.8 3.9 %collective-permute-start.5 = (f32[2,2,3,180]{3,2,1,0:T(4,128)S(1)}, f32[2,2,3,180]{3,2,1,0:T(4,128)S(1)}, u32[]{:S(2)}, u32[]{:S(2)}) collective-permute-start(f32[2,2,3,180]{3,2,1,0:T(4,128)S(1)} %pad_maximum_fusion.9), channel_id=1, source_target_pairs={{0,1},{1,2},{2,3},{3,0},{4,5},{5,6},{6,7},{7,4},{8,9},{9,10},{10,1... | collective-permute-start | bytes 25928 | tf_op jit(solution)/shard_map/ppermute | solution.py:171
  121.8 3.9 %collective-permute-start.3 = (f32[2,2,3,180]{3,2,1,0:T(4,128)S(1)}, f32[2,2,3,180]{3,2,1,0:T(4,128)S(1)}, u32[]{:S(2)}, u32[]{:S(2)}) collective-permute-start(f32[2,2,3,180]{3,2,1,0:T(4,128)S(1)} %pad_maximum_fusion.9), channel_id=1, source_target_pairs={{0,3},{1,0},{2,1},{3,2},{4,7},{5,4},{6,5},{7,6},{8,11},{9,8},{10,9... | collective-permute-start | bytes 25928 | tf_op jit(solution)/shard_map/ppermute | solution.py:171
  156.2 20.0 %all-to-all-start.2 = ((bf16[2,2,3,96,256]{4,1,2,0,3:T(2,128)(2,1)}), bf16[2,2,3,96,256]{4,1,2,0,3:T(2,128)(2,1)}, u32[]{:S(2)}, u32[]{:S(2)}) async-start(bf16[2,2,3,96,256]{4,1,2,0,3:T(2,128)(2,1)} %copy.107), calls=%async_computation.4 | async-start | bytes 1179648 | tf_op jit(solution)/shard_map/all_to_all | solution.py:150
  163.8 47.0 %reduce-scatter.3.cloned.1.call-start = ((), (), s32[]{:S(2)}) async-start(), calls=%async_computation.8 | async-start | bytes 2826240 | tf_op jit(solution)/shard_map/reduce_scatter | solution.py:202
  181.4 2.1 copy-start.5
  183.9 1.0 copy-start.10
  186.2 16.8 %copy-start.13 = (bf16[2,3,180,256]{3,2,1,0:T(8,128)(2,1)S(1)}, bf16[2,3,180,256]{3,2,1,0:T(8,128)(2,1)}, u32[]{:S(2)}) copy-start(bf16[2,3,180,256]{3,2,1,0:T(8,128)(2,1)} %reduce-scatter.5.cloned.1.call-done) | copy-start | bytes 1658884
  186.7 16.2 %copy-start.4 = (bf16[2,3,180,256]{3,0,2,1:T(2,128)(2,1)S(1)}, bf16[2,3,180,256]{3,0,2,1:T(2,128)(2,1)}, u32[]{:S(2)}) copy-start(bf16[2,3,180,256]{3,0,2,1:T(2,128)(2,1)} %param.8) | copy-start | bytes 1658884
  186.7 16.2 %copy-start.7 = (bf16[2,3,180,256]{3,2,1,0:T(8,128)(2,1)S(1)}, bf16[2,3,180,256]{3,2,1,0:T(8,128)(2,1)}, u32[]{:S(2)}) copy-start(bf16[2,3,180,256]{3,2,1,0:T(8,128)(2,1)} %fusion.37) | copy-start | bytes 1658884
  186.7 16.2 %copy-start.9 = (bf16[2,3,180,256]{3,0,2,1:T(2,128)(2,1)S(1)}, bf16[2,3,180,256]{3,0,2,1:T(2,128)(2,1)}, u32[]{:S(2)}) copy-start(bf16[2,3,180,256]{3,0,2,1:T(2,128)(2,1)} %param.9) | copy-start | bytes 1658884
  186.7 16.2 %copy-start.12 = (f32[2,180,96]{2,1,0:T(8,128)S(1)}, f32[2,180,96]{2,1,0:T(8,128)}, u32[]{:S(2)}) copy-start(f32[2,180,96]{2,1,0:T(8,128)} %copy-done.11) | copy-start | bytes 414724
  205.7 4.2 %collective-permute-start.7 = (f32[2,2,3,180]{3,2,1,0:T(4,128)S(1)}, f32[2,2,3,180]{3,2,1,0:T(4,128)S(1)}, u32[]{:S(2)}, u32[]{:S(2)}) collective-permute-start(f32[2,2,3,180]{3,2,1,0:T(4,128)S(1)} %pad_maximum_fusion.10), channel_id=1, source_target_pairs={{0,2},{1,3},{2,0},{3,1},{4,6},{5,7},{6,4},{7,5},{8,10},{9,11},{10,... | collective-permute-start | bytes 25928 | tf_op jit(solution)/shard_map/ppermute | solution.py:171
  206.9 3.8 %collective-permute-start.8 = (f32[2,2,3,180]{3,2,1,0:T(4,128)S(1)}, f32[2,2,3,180]{3,2,1,0:T(4,128)S(1)}, u32[]{:S(2)}, u32[]{:S(2)}) collective-permute-start(f32[2,2,3,180]{3,2,1,0:T(4,128)S(1)} %pad_maximum_fusion.10), channel_id=1, source_target_pairs={{0,1},{1,2},{2,3},{3,0},{4,5},{5,6},{6,7},{7,4},{8,9},{9,10},{10,1... | collective-permute-start | bytes 25928 | tf_op jit(solution)/shard_map/ppermute | solution.py:171
  206.9 3.8 %collective-permute-start.6 = (f32[2,2,3,180]{3,2,1,0:T(4,128)S(1)}, f32[2,2,3,180]{3,2,1,0:T(4,128)S(1)}, u32[]{:S(2)}, u32[]{:S(2)}) collective-permute-start(f32[2,2,3,180]{3,2,1,0:T(4,128)S(1)} %pad_maximum_fusion.10), channel_id=1, source_target_pairs={{0,3},{1,0},{2,1},{3,2},{4,7},{5,4},{6,5},{7,6},{8,11},{9,8},{10,9... | collective-permute-start | bytes 25928 | tf_op jit(solution)/shard_map/ppermute | solution.py:171
Sparse Core Ops, SparseCore 0:
  15.6 35.1 all-gather.2
  78.4 29.8 all-gather.4
  119.4 32.9 reduce-scatter.4
  171.1 30.4 reduce-scatter.2
